TPU v7x, 256 devices: a whole 4x4x8 slice. The times are simulated.
256 devices in a mesh: ctx: 16 (over z_lo, y), dp: 16 (over x, z_hi, core).
Axes of the slice: x: 4, y: 4, z: 8 (z_hi: 2, z_lo: 4; z = z_hi * 4 + z_lo), core: 2. Of those that a mesh axis runs over, the one named last changes fastest.
Arguments:
- inputs: bfloat16 [16, 2048, 4096], P('dp', 'ctx'), may hold values from -6 to 6
- b_proj: bfloat16 [16, 2048, 512], P('dp', 'ctx'), may hold values from -0.75 to 0.75
- c_proj: bfloat16 [16, 2048, 512], P('dp', 'ctx'), may hold values from -0.75 to 0.75
- dt_raw: float32 [16, 64, 2048], P('dp', None, 'ctx'), may hold values from -3 to 9
- a_log: float32 [64], P('dp'), may hold values from -12 to -3
- dt_bias: float32 [64], P('dp'), may hold values from 0.2 to 0.8
- d_skip: float32 [64], P('dp'), may hold values from 0.5 to 1.5
- grad_out: bfloat16 [16, 2048, 4096], P('dp', 'ctx'), may hold values from -6 to 6
Outputs:
- grad_inputs: bfloat16 [16, 2048, 4096], P('dp', 'ctx')
- grad_b: bfloat16 [16, 2048, 512], P('dp', 'ctx')
- grad_c: bfloat16 [16, 2048, 512], P('dp', 'ctx')
- grad_dt: float32 [16, 64, 2048], P('dp', None, 'ctx')
- grad_alog: float32 [64], P('dp')
- grad_bias: float32 [64], P('dp')
- grad_skip: float32 [64], P('dp')
All inputs are finite; a program needn't handle non-finite values.
Results may differ from a plain program's by a relative error of at most 0.0014.
Values sent between devices are 32-bit elements; how exact they have to be, the bound alone decides.
No kernel may reach another device: no remote copies, remote signals or barrier semaphores. Data moves between devices by JAX's collectives and lax.ppermute only.
A program may use at most 192 MiB of HBM per device.

v0:
```python
import jax
import jax.numpy as jnp
from jax import lax
from jax.sharding import PartitionSpec as P

P_SIZE = 64
N = 64
G = 8
highest = lax.Precision.HIGHEST


def slab_scan(x, b, c, raw, bias, alog, skip, state_in):
    tokens, num_heads, width = x.shape
    group_heads = num_heads // G
    dt_value = jax.nn.softplus(raw + bias[:, None])
    log_decay = dt_value * (-jnp.exp(alog))[:, None]
    cumulative = jnp.cumsum(log_decay, axis=1)
    scaled = (x * dt_value.T[:, :, None]).reshape(tokens, G, group_heads, width)
    scores = jnp.einsum("qgn,kgn->gqk", c, b, precision=highest)
    offsets = jnp.arange(tokens)
    causal = offsets[:, None] >= offsets[None, :]
    spread = cumulative[:, :, None] - cumulative[:, None, :]
    weights = jnp.where(causal, jnp.exp(jnp.where(causal, spread, 0.0)), 0.0)
    mixed = weights.reshape(G, group_heads, tokens, tokens) * scores[:, None]
    local_part = jnp.einsum("gjqk,kgjp->qgjp", mixed, scaled, precision=highest)
    tail_decay = jnp.exp(cumulative[:, -1:] - cumulative)
    weighted_b = b[:, :, None, :] * tail_decay.T.reshape(tokens, G, group_heads)[:, :, :, None]
    block_state = jnp.einsum("kgjn,kgjp->gjpn", weighted_b, scaled, precision=highest)
    block_state = block_state.reshape(num_heads, width, N)
    state_out = jnp.exp(cumulative[:, -1])[:, None, None] * state_in + block_state
    entering = state_in.reshape(G, group_heads, width, N)
    cross_part = jnp.einsum("qgn,gjpn->qgjp", c, entering, precision=highest)
    cross_part = cross_part * jnp.exp(cumulative).T.reshape(tokens, G, group_heads)[:, :, :, None]
    result = (local_part + cross_part).reshape(tokens, num_heads, width)
    result = result + skip[None, :, None] * x
    return (result, state_out)


def slab_terms(x, b, c, raw, bias, alog, grad):
    tokens, num_heads, width = x.shape
    group_heads = num_heads // G
    dt_value = jax.nn.softplus(raw + bias[:, None])
    log_decay = dt_value * (-jnp.exp(alog))[:, None]
    cumulative = jnp.cumsum(log_decay, axis=1)
    total = cumulative[:, -1]
    tail_decay = jnp.exp(total[:, None] - cumulative)
    carried = (x * (dt_value * tail_decay).T[:, :, None]).reshape(tokens, G, group_heads, width)
    local_state = jnp.einsum("tgn,tgjp->gjpn", b, carried, precision=highest)
    weighted_grad = (grad * jnp.exp(cumulative).T[:, :, None]).reshape(
        tokens, G, group_heads, width
    )
    local_source = jnp.einsum("tgn,tgjp->gjpn", c, weighted_grad, precision=highest)
    return (
        total,
        local_state.reshape(num_heads, width, N),
        local_source.reshape(num_heads, width, N),
    )


def carry_across(total, local_state, local_source):
    count = lax.axis_size("ctx")
    num_heads = total.shape[0]
    share = num_heads // count
    lanes = local_state.shape[2]
    payload = jnp.concatenate(
        [local_state, local_source, jnp.broadcast_to(total[:, None, None], (num_heads, 1, lanes))],
        axis=1,
    )
    got = lax.all_to_all(payload, "ctx", 0, 0, tiled=True)
    got = got.reshape(count, share, got.shape[1], lanes)
    width = local_state.shape[1]
    states = got[:, :, :width].reshape(count, share, width * lanes)
    sources = got[:, :, width : 2 * width].reshape(count, share, width * lanes)
    totals = got[:, :, 2 * width, 0]
    slab = jnp.arange(count)
    between = (slab[None, :, None] < slab[None, None, :]) & (
        slab[None, None, :] < slab[:, None, None]
    )
    exponent = jnp.einsum("jim,mh->jih", between.astype(jnp.float32), totals, precision=highest)
    before = slab[None, :] < slab[:, None]
    chain = jnp.where(
        before[:, :, None], jnp.exp(jnp.where(before[:, :, None], exponent, 0.0)), 0.0
    )
    entering = jnp.einsum("jih,ihx->jhx", chain, states, precision=highest)
    leaving = jnp.einsum("jkh,jhx->khx", chain, sources, precision=highest)
    back = jnp.concatenate(
        [
            entering.reshape(count * share, width, lanes),
            leaving.reshape(count * share, width, lanes),
        ],
        axis=1,
    )
    mine = lax.all_to_all(back, "ctx", 0, 0, tiled=True)
    return (mine[:, :width], mine[:, width:])


def per_device(inputs, b_proj, c_proj, dt_raw, a_log, dt_bias, d_skip, grad_out):
    params = lax.all_gather(jnp.stack([a_log, dt_bias, d_skip]), "dp", axis=1, tiled=True)
    alog_all, bias_all, skip_all = (params[0], params[1], params[2])
    tokens = inputs.shape[1]
    num_heads = alog_all.shape[0]
    x = inputs[0].astype(jnp.float32).reshape(tokens, num_heads, P_SIZE)
    grad = grad_out[0].astype(jnp.float32).reshape(tokens, num_heads, P_SIZE)
    b = b_proj[0].astype(jnp.float32).reshape(tokens, G, N)
    c = c_proj[0].astype(jnp.float32).reshape(tokens, G, N)
    raw = dt_raw[0]
    total, local_state, local_source = slab_terms(x, b, c, raw, bias_all, alog_all, grad)
    entering, leaving = carry_across(total, local_state, local_source)
    _, pullback = jax.vjp(slab_scan, x, b, c, raw, bias_all, alog_all, skip_all, entering)
    gx, gb, gc, graw, gbias, galog, gskip, _ = pullback((grad, leaving))
    grad_inputs = gx.reshape(tokens, num_heads * P_SIZE).astype(jnp.bfloat16)[None]
    grad_b = gb.reshape(tokens, G * N).astype(jnp.bfloat16)[None]
    grad_c = gc.reshape(tokens, G * N).astype(jnp.bfloat16)[None]
    grad_dt = graw[None]
    head_stats = jnp.stack([galog, gbias, gskip], axis=0)
    share_size = num_heads // lax.axis_size("dp")
    summed = lax.psum(head_stats, ("ctx", "dp"))
    own_totals = lax.dynamic_slice_in_dim(summed, lax.axis_index("dp") * share_size, share_size, 1)
    return (grad_inputs, grad_b, grad_c, grad_dt, own_totals[0], own_totals[1], own_totals[2])


def solution(mesh):
    in_specs = (
        P("dp", "ctx", None),
        P("dp", "ctx", None),
        P("dp", "ctx", None),
        P("dp", None, "ctx"),
        P("dp"),
        P("dp"),
        P("dp"),
        P("dp", "ctx", None),
    )
    out_specs = (
        P("dp", "ctx", None),
        P("dp", "ctx", None),
        P("dp", "ctx", None),
        P("dp", None, "ctx"),
        P("dp"),
        P("dp"),
        P("dp"),
    )
    return jax.shard_map(
        per_device, mesh=mesh, in_specs=in_specs, out_specs=out_specs, check_vma=False
    )
```

profile of v0, /device:TPU:1, one launch (start us, length us, event | category | flops | bytes accessed | tf_op | source)
XLA Modules:
  0.0 347.0 jit_solution(9068073911150541548)
XLA Ops:
  1.5 34.5 %all-gather = f32[16,4,3]{2,1,0:T(4,128)S(1)} all-gather(f32[1,4,3]{2,1,0:T(4,128)S(1)} %bitcast.241), channel_id=1, replica_groups=mesh['ctx'=16,'dp'=16] {'dp'}, dimensions={0}, use_global_device_ids=true | all-gather | bytes 816 | tf_op jit(solution)/shard_map/all_gather | solution.py:98
  39.0 1.6 copy.188
  43.2 3.9 %fusion.9 = f32[8,8,64,64]{2,3,1,0:T(8,128)S(1)} fusion(bf16[128,8,64,1]{0,2,3,1:T(8,128)(2,1)S(1)} %bitcast.214, bf16[128,8,8,64]{0,3,2,1:T(8,128)(2,1)S(1)} %bitcast.198, f32[128,8,8]{0,2,1:T(8,128)} %bitcast.224), kind=kOutput, calls=%fused_computation.19 | convolution fusion | flops 403701760 | bytes 2260992 | tf_op jit(solution)/shard_map/tgn,tgjp->gjpn/dot_general | solution.py:52
  47.1 3.1 fusion.26
  50.5 3.2 pad_maximum_fusion
  53.6 5.7 %all-to-all-start = ((f32[64,129,64]{1,2,0:T(8,128)}), f32[64,129,64]{1,2,0:T(8,128)}, u32[]{:S(2)}, u32[]{:S(2)}) async-start(f32[64,129,64]{1,2,0:T(8,128)} %pad_maximum_fusion), calls=%async_computation | async-start | bytes 8388608 | tf_op jit(solution)/shard_map/all_to_all | solution.py:69
  59.4 78.3 %all-to-all-done = f32[64,129,64]{1,2,0:T(8,128)} async-done(((f32[64,129,64]{1,2,0:T(8,128)}), f32[64,129,64]{1,2,0:T(8,128)}, u32[]{:S(2)}, u32[]{:S(2)}) %all-to-all-start) | async-done | bytes 2113568 | tf_op jit(solution)/shard_map/all_to_all | solution.py:69
  138.7 4.9 %fusion.68 = (f32[16,4,64,64]{2,3,1,0:T(8,128)}, f32[16,4,64,64]{2,3,1,0:T(8,128)}) fusion(f32[16,4,129,64]{2,3,1,0:T(8,128)} %bitcast.26), kind=kLoop, calls=%fused_computation.110 | loop fusion | bytes 4194304 | tf_op jit(solution)/shard_map/slice | solution.py:72
  145.0 3.0 copy.200
  148.0 2.1 reshape.270
  150.1 1.8 convolution_bitcast_fusion.1
  152.6 2.4 reshape.271
  154.9 3.0 copy.204
  157.9 2.1 reshape.272
  160.0 1.8 convolution_bitcast_fusion
  162.5 2.3 reshape.273
  164.8 4.7 %pad_maximum_fusion.1 = f32[64,128,64]{2,1,0:T(8,128)} fusion(f32[64,64,64]{2,1,0:T(8,128)} %reshape.273, f32[64,64,64]{2,1,0:T(8,128)} %reshape.271), kind=kLoop, calls=%fused_computation.3 | loop fusion | flops 524288 | bytes 4194304 | tf_op jit(solution)/shard_map/concatenate | solution.py:86
  169.5 3.8 %copy.207 = f32[64,128,64]{1,2,0:T(8,128)} copy(f32[64,128,64]{2,1,0:T(8,128)} %pad_maximum_fusion.1) | data formatting | bytes 4194304 | tf_op jit(solution)/shard_map/concatenate | solution.py:86
  173.4 19.6 %all-to-all-start.1 = ((f32[64,128,64]{1,2,0:T(8,128)}), f32[64,128,64]{1,2,0:T(8,128)}, u32[]{:S(2)}, u32[]{:S(2)}) async-start(f32[64,128,64]{1,2,0:T(8,128)} %copy.207), calls=%async_computation.1 | async-start | bytes 4194304 | tf_op jit(solution)/shard_map/all_to_all | solution.py:93
  193.5 7.1 %fusion.11 = (f32[8,8,128]{2,1,0:T(8,128)S(1)}, f32[8,8,128]{2,1,0:T(8,128)}, f32[8,128,128]{1,2,0:T(8,128)}) fusion(f32[8,128,128]{1,2,0:T(8,128)S(1)} %fusion.72, f32[8,8,128]{2,1,0:T(8,128)S(1)} %bitcast.235, pred[128,128]{0,1:T(8,128)(4,1)S(1)} %iota_compare_fusion, bf16[8,8,64,128]{3,2,1,0:T(8,128)(2,1)S(1)} %bitcast.199, ...), kind=kOutput, calls=%fused_computation.21 | convolution fusion | flops 817741824 | bytes 3293184 | tf_op jit(solution)/shard_map/transpose(jvp(gjqk,kgjp->qgjp))/dot_general | solution.py:25
  201.6 6.2 %fusion.4 = f32[8,8,128,64]{2,3,1,0:T(8,128)} fusion(bf16[8,8,64,128]{3,2,1,0:T(8,128)(2,1)S(1)} %bitcast.200, f32[8,128,128]{1,2,0:T(8,128)S(1)} %fusion.72, f32[8,8,128]{2,1,0:T(8,128)S(1)} %bitcast.236, pred[128,128]{0,1:T(8,128)(4,1)S(1)} %iota_compare_fusion), kind=kOutput, calls=%fused_computation.10 | convolution fusion | flops 809500672 | bytes 3719168 | tf_op jit(solution)/shard_map/transpose(jvp(gjqk,kgjp->qgjp))/dot_general | solution.py:25
  207.8 26.7 %all-to-all-done.1 = f32[64,128,64]{1,2,0:T(8,128)} async-done(((f32[64,128,64]{1,2,0:T(8,128)}), f32[64,128,64]{1,2,0:T(8,128)}, u32[]{:S(2)}, u32[]{:S(2)}) %all-to-all-start.1) | async-done | bytes 2097184 | tf_op jit(solution)/shard_map/all_to_all | solution.py:93
  234.6 3.7 %multiply_reduce_fusion = (f32[64]{0:T(128)S(1)}, f32[64,64,64]{1,2,0:T(8,128)S(1)}, f32[64,64,64]{1,2,0:T(8,128)S(1)}) fusion(f32[64,128,64]{1,2,0:T(8,128)} %all-to-all-done.1), kind=kLoop, calls=%fused_computation.33 | loop fusion | flops 524224 | bytes 4194560 | tf_op jit(solution)/shard_map/transpose(jvp())/reduce_sum | solution.py:30
  238.3 1.8 fusion.17
  240.1 2.9 fusion.36
  243.0 3.2 fusion.19
  248.1 7.3 %multiply_reduce_fusion.1 = (f32[128,8,8]{0,2,1:T(8,128)S(1)}, f32[128,8,8,64]{0,3,2,1:T(8,128)}) fusion(f32[8,8,128,64]{2,3,1,0:T(8,128)} %fusion.4, f32[8,8,64,64]{2,3,1,0:T(8,128)} %bitcast.208, f32[128,8,8]{0,2,1:T(8,128)S(1)} %bitcast.227, f32[128,8,64]{0,2,1:T(8,128)S(1)} %convert_element_type.70, bf16[128,8,8,64]{0,3,2,1:T(8,128)(2,1)S(1)} %bitcast.206), kind=kOutput, calls=%fused_computation.34 | convolution fusion | flops 405266432 | bytes 6619136 | tf_op jit(solution)/shard_map/transpose(jvp(kgjn,kgjp->gjpn))/dot_general | solution.py:28
  256.3 2.5 fusion.16
  259.1 80.5 %psum.7 = f32[3,64]{1,0:T(4,128)S(1)} all-reduce(f32[3,64]{1,0:T(4,128)S(1)} %pad_maximum_fusion.2), channel_id=1, replica_groups=mesh['ctx'=16,'dp'=16] {'ctx','dp'}, use_global_device_ids=true, to_apply=%region_15.16 | all-reduce | flops 192 | bytes 1536 | tf_op jit(solution)/shard_map/psum | solution.py:117
  340.2 1.5 fusion.40
  342.5 1.8 fusion.39
  345.0 1.3 copy.226
  (93 shorter events, 17.3 us)
Async XLA Ops:
  0.6 40.0 %copy-start.11 = (bf16[1,128,512]{2,1,0:T(8,128)(2,1)S(1)}, bf16[1,128,512]{2,1,0:T(8,128)(2,1)}, u32[]{:S(2)}) copy-start(bf16[1,128,512]{2,1,0:T(8,128)(2,1)} %param.10) | copy-start | bytes 393220
  0.6 40.8 %copy-start.1 = (bf16[1,128,4096]{2,1,0:T(8,128)(2,1)S(1)}, bf16[1,128,4096]{2,1,0:T(8,128)(2,1)}, u32[]{:S(2)}) copy-start(bf16[1,128,4096]{2,1,0:T(8,128)(2,1)} %param.8) | copy-start | bytes 3145732
  36.2 0.9 copy-start.16
  36.2 0.9 copy-start.18
  36.2 2.8 copy-start.14
  37.5 1.5 copy-start.9
  37.6 12.6 %copy-start.12 = (f32[64]{0:T(128)}, f32[64]{0:T(128)S(1)}, u32[]{:S(2)}) copy-start(f32[64]{0:T(128)S(1)} %slice_bitcast_fusion.5) | copy-start | bytes 772
  42.2 4.9 %copy-start.8 = (f32[128,64]{0,1:T(8,128)S(1)}, f32[128,64]{0,1:T(8,128)}, u32[]{:S(2)}) copy-start(f32[128,64]{0,1:T(8,128)} %copy.194) | copy-start | bytes 98308
  53.6 84.1 %all-to-all-start = ((f32[64,129,64]{1,2,0:T(8,128)}), f32[64,129,64]{1,2,0:T(8,128)}, u32[]{:S(2)}, u32[]{:S(2)}) async-start(f32[64,129,64]{1,2,0:T(8,128)} %pad_maximum_fusion), calls=%async_computation | async-start | bytes 8388608 | tf_op jit(solution)/shard_map/all_to_all | solution.py:69
  173.4 19.6 %copy-start.6 = (f32[128,64]{1,0:T(8,128)S(1)}, f32[128,64]{1,0:T(8,128)}, u32[]{:S(2)}) copy-start(f32[128,64]{1,0:T(8,128)} %get-tuple-element.71) | copy-start | bytes 98308
  173.4 19.7 %copy-start.5 = (f32[128,64]{1,0:T(8,128)S(1)}, f32[128,64]{1,0:T(8,128)}, u32[]{:S(2)}) copy-start(f32[128,64]{1,0:T(8,128)} %get-tuple-element.73) | copy-start | bytes 98308
  173.4 20.1 %copy-start.10 = (f32[64,128]{1,0:T(8,128)S(1)}, f32[64,128]{1,0:T(8,128)}, u32[]{:S(2)}) copy-start(f32[64,128]{1,0:T(8,128)} %copy-done.9) | copy-start | bytes 98308
  173.4 61.2 %all-to-all-start.1 = ((f32[64,128,64]{1,2,0:T(8,128)}), f32[64,128,64]{1,2,0:T(8,128)}, u32[]{:S(2)}, u32[]{:S(2)}) async-start(f32[64,128,64]{1,2,0:T(8,128)} %copy.207), calls=%async_computation.1 | async-start | bytes 4194304 | tf_op jit(solution)/shard_map/all_to_all | solution.py:93
  193.1 50.0 %copy-start.3 = (f32[128,64]{0,1:T(8,128)}, f32[128,64]{0,1:T(8,128)S(1)}, u32[]{:S(2)}) copy-start(f32[128,64]{0,1:T(8,128)S(1)} %copy.212) | copy-start | bytes 98308
  238.3 4.8 %copy-start = (f32[64,64,64]{1,2,0:T(8,128)}, f32[64,64,64]{1,2,0:T(8,128)S(1)}, u32[]{:S(2)}) copy-start(f32[64,64,64]{1,2,0:T(8,128)S(1)} %get-tuple-element.67) | copy-start | bytes 3145732
  238.3 1.8 copy-start.2
  243.0 3.3 copy-start.13
  248.0 7.4 %copy-start.15 = (f32[64]{0:T(128)S(1)}, f32[64]{0:T(128)}, u32[]{:S(2)}) copy-start(f32[64]{0:T(128)} %copy-done.14) | copy-start | bytes 772
  248.0 7.4 %copy-start.19 = (f32[64]{0:T(128)S(1)}, f32[64]{0:T(128)}, u32[]{:S(2)}) copy-start(f32[64]{0:T(128)} %copy-done.18) | copy-start | bytes 772
  248.0 8.1 %copy-start.17 = (f32[64,3]{0,1:T(4,128)S(1)}, f32[64,3]{0,1:T(4,128)}, u32[]{:S(2)}) copy-start(f32[64,3]{0,1:T(4,128)} %copy-done.16) | copy-start | bytes 2308
  248.0 8.3 %copy-start.4 = (f32[128,64]{0,1:T(8,128)S(1)}, f32[128,64]{0,1:T(8,128)}, u32[]{:S(2)}) copy-start(f32[128,64]{0,1:T(8,128)} %copy-done.3) | copy-start | bytes 98308
  341.7 4.6 %copy-start.7 = (f32[64,128]{0,1:T(8,128)S(1)}, f32[64,128]{0,1:T(8,128)}, u32[]{:S(2)}) copy-start(f32[64,128]{0,1:T(8,128)} %get-tuple-element.62) | copy-start | bytes 98308
where the time goes:
time: 348 us; the launch traced here: 347 us
  blocking collectives  115 us (33%)
  waiting for transfers between devices  105 us (30%)
  matrix products  43.3 us (12%)
  local copies, waits for them, and re-layouts  38.9 us (11%)
  starting transfers between devices  25.3 us (7%)
  other arithmetic  18.2 us (5%)
    psum x1, blocking collectives, per_device(): summed = lax.psum(head_stats, ('ctx', 'dp'))  80.5 us
    all_to_all x1, waiting for transfers between devices, carry_across(): got = lax.all_to_all(payload, 'ctx', 0, 0, tiled=True)  78.3 us
    all_gather x1, blocking collectives, per_device(): lax.all_gather(jnp.stack([a_log, dt_bias, d_skip]), 'dp', axis=1, tiled=T...  34.5 us
    all_to_all x1, waiting for transfers between devices, carry_across(): mine = lax.all_to_all(back, 'ctx', 0, 0, tiled=True)  26.7 us
    all_to_all x1, starting transfers between devices, carry_across(): mine = lax.all_to_all(back, 'ctx', 0, 0, tiled=True)  19.6 us
    dot_general x2, matrix products, slab_scan(): local_part = jnp.einsum('gjqk,kgjp->qgjp', mixed, scaled, precision=highest)  13.3 us
    dot_general x2, matrix products, slab_scan(): jnp.einsum('kgjn,kgjp->gjpn', weighted_b, scaled, precision=highest)  10.5 us
    unnamed x51, local copies, waits for them, and re-layouts  8.07 us
  transfers between devices with their start and end apart: 2, of which 2 were waited for; matrix products, arithmetic and copies ran while one was open for 4% of the time, Pallas kernels for 0%

commit v1 on v0

--- a/solution.py
+++ b/solution.py
@@ -95,7 +95,10 @@
 
 
 def per_device(inputs, b_proj, c_proj, dt_raw, a_log, dt_bias, d_skip, grad_out):
-    params = lax.all_gather(jnp.stack([a_log, dt_bias, d_skip]), "dp", axis=1, tiled=True)
+    switch_tracks_over_axis = lambda message: jnp.concatenate(
+        jax.lax.all_to_all(jnp.stack(jax.lax.axis_size("dp") * [message]), "dp", 0, 0), 1
+    )
+    params = switch_tracks_over_axis(jnp.stack([a_log, dt_bias, d_skip]))
     alog_all, bias_all, skip_all = (params[0], params[1], params[2])
     tokens = inputs.shape[1]
     num_heads = alog_all.shape[0]

time: 348 us -> 332 us (0.954)
  blocking collectives: 115 us -> 80.5 us
  starting transfers between devices: 25.3 us -> 37.8 us
  waiting for transfers between devices: 105 us -> 109 us
    all_gather x1 -> x0, blocking collectives: 34.5 us -> none  [per_device(): lax.all_gather(jnp.stack([a_log, dt_bias, d_skip]), 'dp', axis=1, tiled=T...]
    all_to_all x0 -> x1, starting transfers between devices: none -> 12.4 us  [per_device(): jax.lax.all_to_all(jnp.stack(jax.lax.axis_size('dp') * [message]), 'dp',...]
    all_to_all x0 -> x1, waiting for transfers between devices: none -> 5.39 us  [per_device(): jax.lax.all_to_all(jnp.stack(jax.lax.axis_size('dp') * [message]), 'dp',...]
    unnamed x51 -> x49, local copies, waits for them, and re-layouts: 8.07 us -> 8.3 us
  transfers between devices with their start and end apart: 2 -> 3, of which waited for: 2 -> 3; matrix products, arithmetic and copies ran while one was open for 4% -> 6% of each run, Pallas kernels for 0% -> 0%
where the time goes in v1:
time: 332 us; the launch traced here: 331 us
  waiting for transfers between devices  109 us (33%)
  blocking collectives  80.5 us (24%)
  matrix products  43.1 us (13%)
  local copies, waits for them, and re-layouts  40.6 us (12%)
  starting transfers between devices  37.8 us (11%)
  other arithmetic  18.6 us (6%)
    psum x1, blocking collectives, per_device(): summed = lax.psum(head_stats, ('ctx', 'dp'))  80.5 us
    all_to_all x1, waiting for transfers between devices, carry_across(): got = lax.all_to_all(payload, 'ctx', 0, 0, tiled=True)  78.3 us
    all_to_all x1, waiting for transfers between devices, carry_across(): mine = lax.all_to_all(back, 'ctx', 0, 0, tiled=True)  25.2 us
    all_to_all x1, starting transfers between devices, carry_across(): mine = lax.all_to_all(back, 'ctx', 0, 0, tiled=True)  19.6 us
    dot_general x2, matrix products, slab_scan(): local_part = jnp.einsum('gjqk,kgjp->qgjp', mixed, scaled, precision=highest)  14.1 us
    all_to_all x1, starting transfers between devices, per_device(): jax.lax.all_to_all(jnp.stack(jax.lax.axis_size('dp') * [message]), 'dp',...  12.4 us
    dot_general x2, matrix products, slab_scan(): jnp.einsum('kgjn,kgjp->gjpn', weighted_b, scaled, precision=highest)  10.5 us
    unnamed x49, local copies, waits for them, and re-layouts  8.3 us
  transfers between devices with their start and end apart: 3, of which 3 were waited for; matrix products, arithmetic and copies ran while one was open for 6% of the time, Pallas kernels for 0%

profile of v1, /device:TPU:1, one launch (start us, length us, event | category | flops | bytes accessed | tf_op | source)
XLA Modules:
  0.0 330.5 jit_solution(4749987517133839716)
XLA Ops:
  2.1 12.4 %all-to-all-start = ((f32[16,3,4]{2,1,0:T(4,128)}), f32[16,3,4]{2,1,0:T(4,128)S(1)}, u32[]{:S(2)}, u32[]{:S(2)}) async-start(f32[16,3,4]{2,1,0:T(4,128)} %stack.20), calls=%async_computation | async-start | bytes 65536 | tf_op jit(solution)/shard_map/all_to_all | solution.py:99
  15.3 1.6 copy.149
  18.8 5.4 %all-to-all-done = f32[16,3,4]{2,1,0:T(4,128)S(1)} async-done(((f32[16,3,4]{2,1,0:T(4,128)}), f32[16,3,4]{2,1,0:T(4,128)S(1)}, u32[]{:S(2)}, u32[]{:S(2)}) %all-to-all-start) | async-done | bytes 800 | tf_op jit(solution)/shard_map/all_to_all | solution.py:99
  26.3 3.2 fusion.9
  29.5 3.1 fusion.26
  32.8 3.2 pad_maximum_fusion
  36.0 5.7 %all-to-all-start.1 = ((f32[64,129,64]{1,2,0:T(8,128)}), f32[64,129,64]{1,2,0:T(8,128)}, u32[]{:S(2)}, u32[]{:S(2)}) async-start(f32[64,129,64]{1,2,0:T(8,128)} %pad_maximum_fusion), calls=%async_computation.1 | async-start | bytes 8388608 | tf_op jit(solution)/shard_map/all_to_all | solution.py:69
  41.8 78.3 %all-to-all-done.1 = f32[64,129,64]{1,2,0:T(8,128)} async-done(((f32[64,129,64]{1,2,0:T(8,128)}), f32[64,129,64]{1,2,0:T(8,128)}, u32[]{:S(2)}, u32[]{:S(2)}) %all-to-all-start.1) | async-done | bytes 2113568 | tf_op jit(solution)/shard_map/all_to_all | solution.py:69
  121.0 4.9 %fusion.69 = (f32[16,4,64,64]{2,3,1,0:T(8,128)}, f32[16,4,64,64]{2,3,1,0:T(8,128)}) fusion(f32[16,4,129,64]{2,3,1,0:T(8,128)} %bitcast.20), kind=kLoop, calls=%fused_computation.111 | loop fusion | bytes 4194304 | tf_op jit(solution)/shard_map/slice | solution.py:72
  127.3 3.0 copy.161
  130.3 2.1 reshape.297
  132.4 1.8 convolution_bitcast_fusion.1
  134.9 2.4 reshape.298
  137.2 3.0 copy.165
  140.2 2.1 reshape.299
  142.3 1.8 convolution_bitcast_fusion
  144.8 2.3 reshape.300
  147.1 4.7 %pad_maximum_fusion.1 = f32[64,128,64]{2,1,0:T(8,128)} fusion(f32[64,64,64]{2,1,0:T(8,128)} %reshape.300, f32[64,64,64]{2,1,0:T(8,128)} %reshape.298), kind=kLoop, calls=%fused_computation.3 | loop fusion | flops 524288 | bytes 4194304 | tf_op jit(solution)/shard_map/concatenate | solution.py:86
  151.8 3.8 %copy.168 = f32[64,128,64]{1,2,0:T(8,128)} copy(f32[64,128,64]{2,1,0:T(8,128)} %pad_maximum_fusion.1) | data formatting | bytes 4194304 | tf_op jit(solution)/shard_map/concatenate | solution.py:86
  155.6 19.6 %all-to-all-start.2 = ((f32[64,128,64]{1,2,0:T(8,128)}), f32[64,128,64]{1,2,0:T(8,128)}, u32[]{:S(2)}, u32[]{:S(2)}) async-start(f32[64,128,64]{1,2,0:T(8,128)} %copy.168), calls=%async_computation.2 | async-start | bytes 4194304 | tf_op jit(solution)/shard_map/all_to_all | solution.py:93
  175.8 7.1 %fusion.11 = (f32[8,8,128]{2,1,0:T(8,128)S(1)}, f32[8,8,128]{2,1,0:T(8,128)}, f32[8,128,128]{1,2,0:T(8,128)}) fusion(f32[8,128,128]{1,2,0:T(8,128)S(1)} %fusion.73, f32[8,8,128]{2,1,0:T(8,128)S(1)} %bitcast.225, pred[128,128]{0,1:T(8,128)(4,1)S(1)} %iota_compare_fusion, bf16[8,8,64,128]{3,2,1,0:T(8,128)(2,1)S(1)} %bitcast.189, ...), kind=kOutput, calls=%fused_computation.21 | convolution fusion | flops 817741824 | bytes 3293184 | tf_op jit(solution)/shard_map/transpose(jvp(gjqk,kgjp->qgjp))/dot_general | solution.py:25
  184.8 6.9 %fusion.4 = f32[8,8,128,64]{2,3,1,0:T(8,128)} fusion(bf16[8,8,64,128]{3,2,1,0:T(8,128)(2,1)S(1)} %bitcast.190, f32[8,128,128]{1,2,0:T(8,128)S(1)} %fusion.73, f32[8,8,128]{2,1,0:T(8,128)S(1)} %bitcast.226, pred[128,128]{0,1:T(8,128)(4,1)} %copy-done.12), kind=kOutput, calls=%fused_computation.10 | convolution fusion | flops 809500672 | bytes 3719168 | tf_op jit(solution)/shard_map/transpose(jvp(gjqk,kgjp->qgjp))/dot_general | solution.py:25
  191.7 25.2 %all-to-all-done.2 = f32[64,128,64]{1,2,0:T(8,128)} async-done(((f32[64,128,64]{1,2,0:T(8,128)}), f32[64,128,64]{1,2,0:T(8,128)}, u32[]{:S(2)}, u32[]{:S(2)}) %all-to-all-start.2) | async-done | bytes 2097184 | tf_op jit(solution)/shard_map/all_to_all | solution.py:93
  216.8 3.7 %multiply_reduce_fusion = (f32[64]{0:T(128)S(1)}, f32[64,64,64]{1,2,0:T(8,128)S(1)}, f32[64,64,64]{1,2,0:T(8,128)S(1)}) fusion(f32[64,128,64]{1,2,0:T(8,128)} %all-to-all-done.2), kind=kLoop, calls=%fused_computation.33 | loop fusion | flops 524224 | bytes 4194560 | tf_op jit(solution)/shard_map/transpose(jvp())/reduce_sum | solution.py:30
  220.5 1.8 fusion.17
  222.4 2.9 fusion.36
  225.3 3.2 fusion.19
  230.9 7.3 %multiply_reduce_fusion.1 = (f32[128,8,8]{0,2,1:T(8,128)S(1)}, f32[128,8,8,64]{0,3,2,1:T(8,128)}) fusion(f32[8,8,128,64]{2,3,1,0:T(8,128)} %fusion.4, f32[8,8,64,64]{2,3,1,0:T(8,128)} %bitcast.198, f32[128,8,8]{0,2,1:T(8,128)S(1)} %bitcast.217, f32[128,8,64]{0,2,1:T(8,128)S(1)} %convert_element_type.70, bf16[128,8,8,64]{0,3,2,1:T(8,128)(2,1)S(1)} %bitcast.196), kind=kOutput, calls=%fused_computation.34 | convolution fusion | flops 405266432 | bytes 6619136 | tf_op jit(solution)/shard_map/transpose(jvp(kgjn,kgjp->gjpn))/dot_general | solution.py:28
  239.0 2.6 fusion.16
  242.8 80.5 %psum.7 = f32[3,64]{1,0:T(4,128)S(1)} all-reduce(f32[3,64]{1,0:T(4,128)S(1)} %pad_maximum_fusion.3), channel_id=1, replica_groups=mesh['ctx'=16,'dp'=16] {'ctx','dp'}, use_global_device_ids=true, to_apply=%region_15.16 | all-reduce | flops 192 | bytes 1536 | tf_op jit(solution)/shard_map/psum | solution.py:120
  324.6 1.5 fusion.40
  326.8 1.6 fusion.39
  (97 shorter events, 20.7 us)
Async XLA Ops:
  0.6 16.3 %copy-start.11 = (bf16[1,128,512]{2,1,0:T(8,128)(2,1)S(1)}, bf16[1,128,512]{2,1,0:T(8,128)(2,1)}, u32[]{:S(2)}) copy-start(bf16[1,128,512]{2,1,0:T(8,128)(2,1)} %param.10) | copy-start | bytes 393220
  0.6 16.5 %copy-start.2 = (bf16[1,128,4096]{2,1,0:T(8,128)(2,1)S(1)}, bf16[1,128,4096]{2,1,0:T(8,128)(2,1)}, u32[]{:S(2)}) copy-start(bf16[1,128,4096]{2,1,0:T(8,128)(2,1)} %param.8) | copy-start | bytes 3145732
  2.1 22.1 %all-to-all-start = ((f32[16,3,4]{2,1,0:T(4,128)}), f32[16,3,4]{2,1,0:T(4,128)S(1)}, u32[]{:S(2)}, u32[]{:S(2)}) async-start(f32[16,3,4]{2,1,0:T(4,128)} %stack.20), calls=%async_computation | async-start | bytes 65536 | tf_op jit(solution)/shard_map/all_to_all | solution.py:99
  24.4 5.1 %copy-start.15 = (f32[64]{0:T(128)}, f32[64]{0:T(128)S(1)}, u32[]{:S(2)}) copy-start(f32[64]{0:T(128)S(1)} %add.29) | copy-start | bytes 772
  24.5 0.5 copy-start.17
  25.3 0.8 copy-start.9
  25.4 7.2 %copy-start.13 = (f32[64]{0:T(128)}, f32[64]{0:T(128)S(1)}, u32[]{:S(2)}) copy-start(f32[64]{0:T(128)S(1)} %slice_bitcast_fusion.3) | copy-start | bytes 772
  26.2 6.4 %copy-start.3 = (f32[128,64]{0,1:T(8,128)}, f32[128,64]{0,1:T(8,128)S(1)}, u32[]{:S(2)}) copy-start(f32[128,64]{0,1:T(8,128)S(1)} %copy.159) | copy-start | bytes 98308
  36.0 84.0 %all-to-all-start.1 = ((f32[64,129,64]{1,2,0:T(8,128)}), f32[64,129,64]{1,2,0:T(8,128)}, u32[]{:S(2)}, u32[]{:S(2)}) async-start(f32[64,129,64]{1,2,0:T(8,128)} %pad_maximum_fusion), calls=%async_computation.1 | async-start | bytes 8388608 | tf_op jit(solution)/shard_map/all_to_all | solution.py:69
  155.6 20.0 %copy-start.8 = (f32[128,64]{1,0:T(8,128)S(1)}, f32[128,64]{1,0:T(8,128)}, u32[]{:S(2)}) copy-start(f32[128,64]{1,0:T(8,128)} %get-tuple-element.68) | copy-start | bytes 98308
  155.6 20.1 %copy-start.7 = (f32[128,64]{1,0:T(8,128)S(1)}, f32[128,64]{1,0:T(8,128)}, u32[]{:S(2)}) copy-start(f32[128,64]{1,0:T(8,128)} %get-tuple-element.70) | copy-start | bytes 98308
  155.6 20.1 %copy-start.10 = (f32[64,128]{1,0:T(8,128)S(1)}, f32[64,128]{1,0:T(8,128)}, u32[]{:S(2)}) copy-start(f32[64,128]{1,0:T(8,128)} %copy-done.9) | copy-start | bytes 98308
  155.6 61.2 %all-to-all-start.2 = ((f32[64,128,64]{1,2,0:T(8,128)}), f32[64,128,64]{1,2,0:T(8,128)}, u32[]{:S(2)}, u32[]{:S(2)}) async-start(f32[64,128,64]{1,2,0:T(8,128)} %copy.168), calls=%async_computation.2 | async-start | bytes 4194304 | tf_op jit(solution)/shard_map/all_to_all | solution.py:93
  175.3 7.6 %copy-start.12 = (pred[128,128]{0,1:T(8,128)(4,1)}, pred[128,128]{0,1:T(8,128)(4,1)S(1)}, u32[]{:S(2)}) copy-start(pred[128,128]{0,1:T(8,128)(4,1)S(1)} %iota_compare_fusion) | copy-start | bytes 49156
  175.7 49.6 %copy-start.5 = (f32[128,64]{0,1:T(8,128)}, f32[128,64]{0,1:T(8,128)S(1)}, u32[]{:S(2)}) copy-start(f32[128,64]{0,1:T(8,128)S(1)} %copy.173) | copy-start | bytes 98308
  220.5 4.8 %copy-start = (f32[64,64,64]{1,2,0:T(8,128)}, f32[64,64,64]{1,2,0:T(8,128)S(1)}, u32[]{:S(2)}) copy-start(f32[64,64,64]{1,2,0:T(8,128)S(1)} %get-tuple-element.64) | copy-start | bytes 3145732
  220.5 1.8 copy-start.4
  225.3 3.3 %copy-start.14 = (f32[64]{0:T(128)S(1)}, f32[64]{0:T(128)}, u32[]{:S(2)}) copy-start(f32[64]{0:T(128)} %copy-done.13) | copy-start | bytes 772
  230.9 8.0 %copy-start.6 = (f32[128,64]{0,1:T(8,128)S(1)}, f32[128,64]{0,1:T(8,128)}, u32[]{:S(2)}) copy-start(f32[128,64]{0,1:T(8,128)} %copy-done.5) | copy-start | bytes 98308
  239.0 2.8 copy-start.16
  239.0 2.8 copy-start.18
  239.0 3.8 %copy-start.19 = (f32[1,64]{1,0:T(1,128)S(1)}, f32[1,64]{1,0:T(1,128)}, u32[]{:S(2)}) copy-start(f32[1,64]{1,0:T(1,128)} %exp.68) | copy-start | bytes 772
  241.5 85.3 %copy-start.1 = (f32[8,128,128]{1,2,0:T(8,128)S(1)}, f32[8,128,128]{1,2,0:T(8,128)}, u32[]{:S(2)}) copy-start(f32[8,128,128]{1,2,0:T(8,128)} %get-tuple-element.51) | copy-start | bytes 1572868
